TPU v7x, 32 devices: a whole 2x2x4 slice. The times are simulated.
32 devices in a mesh: crop: 8 (over z, y), head: 4 (over x, core).
Axes of the slice: x: 2, y: 2, z: 4, core: 2. Of those that a mesh axis runs over, the one named last changes fastest.
Arguments:
- global_rows: bfloat16 [4096, 4096], P('crop', 'head'), may hold values from -6 to 6
- crop_tokens: bfloat16 [8192, 4096], P('crop', 'head'), may hold values from -6 to 6
- query_weight: bfloat16 [4096, 4096], P('crop', 'head'), may hold values from -0.125 to 0.125
- key_weight: bfloat16 [4096, 4096], P('crop', 'head'), may hold values from -0.125 to 0.125
- value_weight: bfloat16 [4096, 4096], P('crop', 'head'), may hold values from -0.09375 to 0.09375
- fetch_slots: int32 [8, 8, 2], P('crop'), may hold values from 0 to 63
- region_slots: int32 [128, 8], P('crop'), may hold values from 0 to 15, as said below
- region_len: int32 [128], P('crop'), may hold values from 4 to 8
Outputs:
- attended: bfloat16 [4096, 4096], P('crop', 'head')
Inputs may be any that keep to these rules, and one draw needn't show every extreme that they name: `fetch_slots`: entry [s, o, c] numbers one of the 64 crop blocks of index s of crop. `region_slots`: the blocks listed for one page-row are distinct; the lists of the 16 page-rows of one index of crop together name all 16 delivered blocks. page-row r uses its first region_len[r] listed blocks.
All inputs are finite; a program needn't handle non-finite values.
Results may differ from a plain program's by a relative error of at most 0.008.
Values may be sent and summed in bfloat16 or wider, within the bound.
No kernel may reach another device: no remote copies, remote signals or barrier semaphores. Data moves between devices by JAX's collectives and lax.ppermute only.
A program may use at most 128 MiB of HBM per device.

v0:
```python
import jax
import jax.numpy as jnp
from jax import lax
from jax.sharding import PartitionSpec as P

HD = 128
CT = 16
CAP = 2
NB = 8
GR = 32


def add_rows(left, piece):
    return jnp.dot(left, piece, preferred_element_type=jnp.float32)


def body(
    global_rows,
    crop_tokens,
    query_weight,
    key_weight,
    value_weight,
    fetch_slots,
    region_slots,
    region_len,
):
    width = key_weight.shape[1]
    heads_here = width // HD
    ncrop = lax.axis_size("crop")
    rows_here = region_slots.shape[0]
    queries_in = lax.all_gather(global_rows, "head", axis=1, tiled=True)
    query = add_rows(queries_in, lax.all_gather(query_weight, "crop", axis=0, tiled=True)).astype(
        jnp.bfloat16
    )
    picks = fetch_slots[0]
    tokens_all = lax.all_gather(crop_tokens, "head", axis=1, tiled=True)

    def add_one(piece):
        return add_rows(tokens_all, piece)

    keys_full = add_one(lax.all_gather(key_weight, "crop", axis=0, tiled=True))
    vals_full = add_one(lax.all_gather(value_weight, "crop", axis=0, tiled=True))
    packed = jnp.concatenate(
        [keys_full.astype(jnp.bfloat16), vals_full.astype(jnp.bfloat16)], axis=1
    )
    packed = packed.reshape(-1, CT, 2 * width)
    outgoing = packed[picks]
    incoming = lax.all_to_all(outgoing, "crop", split_axis=0, concat_axis=0, tiled=True)
    slotted = incoming.reshape(ncrop * CAP, CT, 2 * width)
    listed = slotted[region_slots].reshape(rows_here, NB * CT, 2 * width)
    keys_row = listed[:, :, :width].reshape(rows_here, NB * CT, heads_here, HD)
    vals_row = listed[:, :, width:].reshape(rows_here, NB * CT, heads_here, HD)
    query_row = query.reshape(rows_here, GR, heads_here, HD)
    scale = 1.0 / HD**0.5
    scores = (
        jnp.einsum("rghe,rkhe->rhgk", query_row, keys_row, preferred_element_type=jnp.float32)
        * scale
    )
    used = (jnp.arange(NB * CT, dtype=jnp.int32) // CT)[None, :] < region_len[:, None]
    scores = jnp.where(used[:, None, None, :], scores, jnp.float32(-1e30))
    top = jnp.max(scores, axis=-1, keepdims=True)
    expo = jnp.exp(scores - top)
    weights = (expo / jnp.sum(expo, axis=-1, keepdims=True)).astype(jnp.bfloat16)
    result = jnp.einsum("rhgk,rkhe->rghe", weights, vals_row, preferred_element_type=jnp.float32)
    return result.astype(jnp.bfloat16).reshape(rows_here * GR, width)


def solution(mesh):
    placed = (
        P("crop", "head"),
        P("crop", "head"),
        P("crop", "head"),
        P("crop", "head"),
        P("crop", "head"),
        P("crop", None, None),
        P("crop", None),
        P("crop"),
    )
    return jax.shard_map(
        body, mesh=mesh, in_specs=placed, out_specs=P("crop", "head"), check_vma=False
    )
```

profile of v0, /device:TPU:0, one launch (start us, length us, event | category | flops | bytes accessed | tf_op | source)
XLA Modules:
  0.0 549.0 jit_solution(13589215673044014440)
XLA Ops:
  6.5 0.0 copy-start.2
  6.5 0.0 copy-start.1
  6.5 0.0 all-gather.6.cloned.1.call-start
  6.5 0.7 all-gather.6.cloned.1.call-update
  7.3 0.0 all-gather.8.cloned.1.call-start
  7.3 0.7 all-gather.8.cloned.1.call-update
  8.0 0.0 all-gather.10.cloned.1.call-start
  8.1 0.7 all-gather.10.cloned.1.call-update
  8.7 0.0 all-gather.12.cloned.1.call-start
  8.8 0.5 all-gather.12.cloned.1.call-update
  9.3 0.0 all-gather.14.cloned.1.call-start
  9.4 0.5 all-gather.14.cloned.1.call-update
  9.9 0.0 copy-done.2
  9.9 0.1 copy.13
  10.0 0.1 reshape.96
  10.1 0.0 copy-done.1
  10.1 0.1 copy.14
  10.2 0.1 reshape.104
  10.3 59.6 %all-gather.6.cloned.1.call-done = bf16[1024,4096]{1,0:T(8,128)(2,1)} async-done(((bf16[1024,1024]{1,0:T(8,128)(2,1)}), bf16[1024,4096]{1,0:T(8,128)(2,1)}) %all-gather.6.cloned.1.call-update) | async-done | bytes 8388624 | tf_op jit(solution)/shard_map/all_gather | solution.py:36
  69.9 127.1 %all-gather.8.cloned.1.call-done = bf16[4096,1024]{1,0:T(8,128)(2,1)} async-done(((bf16[512,1024]{1,0:T(8,128)(2,1)}), bf16[4096,1024]{1,0:T(8,128)(2,1)}) %all-gather.8.cloned.1.call-update) | async-done | bytes 8388624 | tf_op jit(solution)/shard_map/all_gather | solution.py:41
  197.0 13.7 %convolution_convert_fusion.1 = bf16[1024,1024]{0,1:T(8,128)(2,1)S(1)} fusion(bf16[1024,4096]{1,0:T(8,128)(2,1)} %all-gather.6.cloned.1.call-done, bf16[4096,1024]{1,0:T(8,128)(2,1)} %all-gather.8.cloned.1.call-done), kind=kOutput, calls=%fused_computation.8 | convolution fusion | flops 8590983168 | bytes 18874368 | tf_op jit(solution)/shard_map/dot_general | solution.py:14
  210.8 111.5 %all-gather.10.cloned.1.call-done = bf16[4096,1024]{1,0:T(8,128)(2,1)} async-done(((bf16[512,1024]{1,0:T(8,128)(2,1)}), bf16[4096,1024]{1,0:T(8,128)(2,1)}) %all-gather.10.cloned.1.call-update) | async-done | bytes 8388624 | tf_op jit(solution)/shard_map/all_gather | solution.py:42
  322.3 13.7 %convolution_convert_fusion = bf16[1024,1024]{0,1:T(8,128)(2,1)S(1)} fusion(bf16[1024,4096]{1,0:T(8,128)(2,1)} %all-gather.6.cloned.1.call-done, bf16[4096,1024]{1,0:T(8,128)(2,1)} %all-gather.10.cloned.1.call-done), kind=kOutput, calls=%fused_computation.7 | convolution fusion | flops 8590983168 | bytes 18874368 | tf_op jit(solution)/shard_map/dot_general | solution.py:14
  336.1 2.4 pad_maximum_fusion
  338.5 6.6 %copy.12 = bf16[1024,2048]{1,0:T(8,128)(2,1)} copy(bf16[1024,2048]{0,1:T(8,128)(2,1)} %pad_maximum_fusion) | data formatting | bytes 8388608 | tf_op jit(solution)/shard_map/concatenate | solution.py:43
  345.1 0.0 copy-start.3
  345.1 3.8 gather_fusion
  348.9 3.7 all-to-all-start
  352.6 0.0 copy-done.3
  352.6 0.1 broadcast_compare_fusion
  352.7 3.7 all-gather.12.cloned.1.call-done
  356.4 133.9 %all-gather.14.cloned.1.call-done = bf16[4096,1024]{1,0:T(8,128)(2,1)} async-done(((bf16[512,1024]{1,0:T(8,128)(2,1)}), bf16[4096,1024]{1,0:T(8,128)(2,1)}) %all-gather.14.cloned.1.call-update) | async-done | bytes 8388624 | tf_op jit(solution)/shard_map/all_gather | solution.py:32
  490.3 9.1 %fusion.3 = bf16[64,8,8,128]{3,1,2,0:T(8,128)(2,1)S(1)} fusion(bf16[512,4096]{1,0:T(8,128)(2,1)} %all-gather.12.cloned.1.call-done, bf16[4096,1024]{1,0:T(8,128)(2,1)} %all-gather.14.cloned.1.call-done), kind=kOutput, calls=%fused_computation.13 | convolution fusion | flops 4295491584 | bytes 13631488 | tf_op jit(solution)/shard_map/dot_general | solution.py:14
  499.4 0.3 copy.23
  499.7 0.0 all-to-all-done
  499.7 6.2 %gather_fusion.1 = bf16[128,16,2048]{2,1,0:T(8,128)(2,1)} fusion(bf16[16,16,2048]{2,1,0:T(8,128)(2,1)S(1)} %bitcast.29, s32[1024]{0:T(1024)S(1)} %pad_clamp_fusion), kind=kCustom, calls=%fused_computation.1 | custom fusion | bytes 16777728 | tf_op jit(solution)/shard_map/gather | solution.py:50
  506.0 6.0 %fusion.17 = (bf16[16,128,1024]{2,1,0:T(8,128)(2,1)}, bf16[16,128,1024]{2,1,0:T(8,128)(2,1)}) fusion(bf16[16,128,2048]{2,1,0:T(8,128)(2,1)} %bitcast.30), kind=kLoop, calls=%fused_computation.35 | loop fusion | bytes 16777216 | tf_op jit(solution)/shard_map/slice | solution.py:51
  512.0 6.4 %copy.16 = bf16[16,128,1024]{1,2,0:T(8,128)(2,1)} copy(bf16[16,128,1024]{2,1,0:T(8,128)(2,1)} %get-tuple-element.5) | data formatting | bytes 8388608 | tf_op jit(solution)/shard_map/slice | solution.py:51
  518.4 6.4 %copy.15 = bf16[16,128,1024]{1,2,0:T(8,128)(2,1)} copy(bf16[16,128,1024]{2,1,0:T(8,128)(2,1)} %get-tuple-element.6) | data formatting | bytes 8388608 | tf_op jit(solution)/shard_map/slice | solution.py:52
  524.8 3.4 fusion.4
  528.2 0.0 copy-start
  528.2 1.3 copy-done
  529.5 1.2 fusion.18
  530.7 10.1 %fusion.2 = bf16[16,32,8,128]{3,1,2,0:T(8,128)(2,1)S(1)} fusion(bf16[16,128,8,128]{1,3,2,0:T(8,128)(2,1)} %bitcast.34, f32[16,8,32]{2,1,0:T(8,128)S(1)} %fusion.18, f32[16,8,32,128]{3,2,1,0:T(8,128)} %copy-done, pred[16,128]{1,0:T(8,128)(4,1)S(1)} %broadcast_compare_fusion), kind=kOutput, calls=%fused_computation.12 | convolution fusion | flops 137367680 | bytes 7358464 | tf_op jit(solution)/shard_map/rhgk,rkhe->rghe/dot_general | solution.py:64
  540.8 0.5 copy.20
  541.2 1.2 copy.28
  (5 shorter events, 0.0 us)
Async XLA Ops:
  6.5 3.4 copy-start.2
  6.5 3.6 copy-start.1
  6.5 63.4 %all-gather.6.cloned.1.call-start = ((), (), s32[]{:S(2)}) async-start(), calls=%async_computation.1 | async-start | bytes 10485760 | tf_op jit(solution)/shard_map/all_gather | solution.py:36
  7.3 189.8 %all-gather.8.cloned.1.call-start = ((), (), s32[]{:S(2)}) async-start(), calls=%async_computation.2 | async-start | bytes 9437184 | tf_op jit(solution)/shard_map/all_gather | solution.py:41
  8.0 314.3 %all-gather.10.cloned.1.call-start = ((), (), s32[]{:S(2)}) async-start(), calls=%async_computation.3 | async-start | bytes 9437184 | tf_op jit(solution)/shard_map/all_gather | solution.py:42
  8.7 347.7 %all-gather.12.cloned.1.call-start = ((), (), s32[]{:S(2)}) async-start(), calls=%async_computation.4 | async-start | bytes 5242880 | tf_op jit(solution)/shard_map/all_gather | solution.py:31
  9.3 481.0 %all-gather.14.cloned.1.call-start = ((), (), s32[]{:S(2)}) async-start(), calls=%async_computation.5 | async-start | bytes 9437184 | tf_op jit(solution)/shard_map/all_gather | solution.py:32
  345.1 7.5 %copy-start.3 = (s32[16]{0:T(128)S(1)}, s32[16]{0:T(128)}, u32[]{:S(2)}) copy-start(s32[16]{0:T(128)} %param.15) | copy-start | bytes 196
  348.9 150.9 %all-to-all-start = ((bf16[8,2,16,2048]{3,2,1,0:T(8,128)(2,1)}), bf16[8,2,16,2048]{3,2,1,0:T(8,128)(2,1)S(1)}, u32[]{:S(2)}, u32[]{:S(2)}) async-start(bf16[8,2,16,2048]{3,2,1,0:T(8,128)(2,1)} %bitcast.2), calls=%async_computation | async-start | bytes 2097152 | tf_op jit(solution)/shard_map/all_to_all | solution.py:48
  528.2 1.3 copy-start
Sparse Core Ops, SparseCore 0:
  8.9 60.9 all-gather.5
  72.1 124.9 all-gather.7
  199.2 123.1 all-gather.9
  323.7 32.6 all-gather.11
  358.4 131.8 all-gather.13
where the time goes:
time: 550 us; the launch traced here: 549 us
  waiting for transfers between devices  439 us (80%)
  matrix products  50.1 us (9%)
  local copies, waits for them, and re-layouts  39.1 us (7%)
  between operations  13.3 us (2%)
    all_gather x1, waiting for transfers between devices, body(): lax.all_gather(query_weight, 'crop', axis=0, tiled=True)  134 us
    all_gather x1, waiting for transfers between devices, body(): keys_full = add_one(lax.all_gather(key_weight, 'crop', axis=0, tiled=True))  127 us
    all_gather x1, waiting for transfers between devices, body(): lax.all_gather(value_weight, 'crop', axis=0, tiled=True)  112 us
    all_gather x1, waiting for transfers between devices, body(): tokens_all = lax.all_gather(crop_tokens, 'head', axis=1, tiled=True)  59.6 us
    dot_general x3, matrix products, add_rows(): return jnp.dot(left, piece, preferred_element_type=jnp.float32)  36.6 us
    slice x2, local copies, waits for them, and re-layouts, body(): keys_row = listed[:, :, :width].reshape(rows_here, NB * CT, heads_here, HD)  12.4 us
  transfers between devices with their start and end apart: 6, of which 5 were waited for; matrix products, arithmetic and copies ran while one was open for 9% of the time, Pallas kernels for 0%

commit v1 on v0

--- a/solution.py
+++ b/solution.py
@@ -8,6 +8,27 @@
 CAP = 2
 NB = 8
 GR = 32
+
+
+def gather_around(x, axis, dim):
+    peers, position, width = (lax.axis_size(axis), lax.axis_index(axis), x.shape[dim])
+    right = [(i, (i + 1) % peers) for i in range(peers)]
+    behind = [(i, (i - 1) % peers) for i in range(peers)]
+    result = jnp.zeros((*x.shape[:dim], peers * width, *x.shape[dim + 1 :]), x.dtype)
+    result = lax.dynamic_update_slice_in_dim(result, x, position * width, axis=dim)
+    from_left = from_right = x
+    halfway = peers // 2
+    for hop in range(1, halfway + 1):
+        from_left = lax.ppermute(from_left, axis, right)
+        result = lax.dynamic_update_slice_in_dim(
+            result, from_left, (position - hop) % peers * width, axis=dim
+        )
+        if hop < peers - halfway:
+            from_right = lax.ppermute(from_right, axis, behind)
+            result = lax.dynamic_update_slice_in_dim(
+                result, from_right, (position + hop) % peers * width, axis=dim
+            )
+    return result
 
 
 def add_rows(left, piece):
@@ -29,9 +50,7 @@
     ncrop = lax.axis_size("crop")
     rows_here = region_slots.shape[0]
     queries_in = lax.all_gather(global_rows, "head", axis=1, tiled=True)
-    query = add_rows(queries_in, lax.all_gather(query_weight, "crop", axis=0, tiled=True)).astype(
-        jnp.bfloat16
-    )
+    query = add_rows(queries_in, gather_around(query_weight, "crop", 0)).astype(jnp.bfloat16)
     picks = fetch_slots[0]
     tokens_all = lax.all_gather(crop_tokens, "head", axis=1, tiled=True)
 

time: 550 us -> 494 us (0.90)
  waiting for transfers between devices: 439 us -> 343 us
  starting transfers between devices: 3.89 us -> 24.5 us
  local copies, waits for them, and re-layouts: 39.1 us -> 58.7 us
    ppermute x0 -> x7, waiting for transfers between devices: none -> 137 us  [the longest x4 137 us: gather_around(): from_left = lax.ppermute(from_left, axis, right)]
    all_gather x1 -> x0, waiting for transfers between devices: 134 us -> none  [body(): lax.all_gather(query_weight, 'crop', axis=0, tiled=True)]
    all_gather x1, waiting for transfers between devices: 59.6 us -> 0.01 us  [body(): tokens_all = lax.all_gather(crop_tokens, 'head', axis=1, tiled=True)]
    all_gather x1, waiting for transfers between devices: 112 us -> 84.1 us  [body(): lax.all_gather(value_weight, 'crop', axis=0, tiled=True)]
    ppermute x0 -> x7, starting transfers between devices: none -> 20.6 us  [the longest x4 11.4 us: gather_around(): from_left = lax.ppermute(from_left, axis, right)]
    all_gather x1, waiting for transfers between devices: 127 us -> 112 us  [body(): keys_full = add_one(lax.all_gather(key_weight, 'crop', axis=0, tiled=True))]
    dynamic_update_slice x0 -> x8, local copies, waits for them, and re-layouts: none -> 14.7 us  [the longest x4 7.93 us: gather_around(): lax.dynamic_update_slice_in_dim(result, from_left, (position - hop) % pee...]
    all_to_all x1, waiting for transfers between devices: 0.01 us -> 7.5 us  [body(): lax.all_to_all(outgoing, 'crop', split_axis=0, concat_axis=0, tiled=True)]
  transfers between devices with their start and end apart: 6 -> 12, of which waited for: 5 -> 6; matrix products, arithmetic and copies ran while one was open for 9% -> 14% of each run, Pallas kernels for 0% -> 0%
where the time goes in v1:
time: 494 us; the launch traced here: 493 us
  waiting for transfers between devices  343 us (69%)
  local copies, waits for them, and re-layouts  58.7 us (12%)
  matrix products  50.1 us (10%)
  starting transfers between devices  24.5 us (5%)
  between operations  13.3 us (3%)
    ppermute x4, waiting for transfers between devices, gather_around(): from_left = lax.ppermute(from_left, axis, right)  137 us
    all_gather x1, waiting for transfers between devices, body(): keys_full = add_one(lax.all_gather(key_weight, 'crop', axis=0, tiled=True))  112 us
    all_gather x1, waiting for transfers between devices, body(): lax.all_gather(value_weight, 'crop', axis=0, tiled=True)  84.1 us
    dot_general x3, matrix products, add_rows(): return jnp.dot(left, piece, preferred_element_type=jnp.float32)  36.6 us
    slice x2, local copies, waits for them, and re-layouts, body(): keys_row = listed[:, :, :width].reshape(rows_here, NB * CT, heads_here, HD)  12.5 us
    ppermute x4, starting transfers between devices, gather_around(): from_left = lax.ppermute(from_left, axis, right)  11.4 us
    dot_general x1, matrix products, body(): jnp.einsum('rhgk,rkhe->rghe', weights, vals_row, preferred_element_type=j...  10.1 us
  transfers between devices with their start and end apart: 12, of which 6 were waited for; matrix products, arithmetic and copies ran while one was open for 14% of the time, Pallas kernels for 0%

profile of v1, /device:TPU:0, one launch (start us, length us, event | category | flops | bytes accessed | tf_op | source)
XLA Modules:
  0.0 493.1 jit_solution(6317913797107463924)
XLA Ops:
  6.5 0.7 all-gather.5.cloned.1.call-update
  7.3 0.7 all-gather.9.cloned.1.call-update
  8.1 0.7 all-gather.7.cloned.1.call-update
  8.8 3.0 collective-permute-start
  11.8 3.1 collective-permute-start.1
  14.9 41.8 %collective-permute-done = bf16[512,1024]{1,0:T(8,128)(2,1)} collective-permute-done((bf16[512,1024]{1,0:T(8,128)(2,1)S(1)}, bf16[512,1024]{1,0:T(8,128)(2,1)}, u32[]{:S(2)}, u32[]{:S(2)}) %collective-permute-start) | collective-permute-done | bytes 1048608 | tf_op jit(solution)/shard_map/ppermute | solution.py:22
  56.7 2.6 collective-permute-start.2
  59.4 3.1 collective-permute-start.3
  62.5 52.4 %collective-permute-done.2 = bf16[512,1024]{1,0:T(8,128)(2,1)S(1)} collective-permute-done((bf16[512,1024]{1,0:T(8,128)(2,1)}, bf16[512,1024]{1,0:T(8,128)(2,1)S(1)}, u32[]{:S(2)}, u32[]{:S(2)}) %collective-permute-start.2) | collective-permute-done | bytes 1048608 | tf_op jit(solution)/shard_map/ppermute | solution.py:22
  114.9 2.4 collective-permute-start.4
  117.2 0.1 copy.13
  117.3 0.1 reshape.96
  117.5 0.1 reshape.104
  117.7 4.3 broadcast_in_dim.26
  122.0 1.1 constant_dynamic-update-slice_fusion.7
  123.1 0.1 broadcast_compare_fusion
  123.2 2.3 constant_dynamic-update-slice_fusion.6
  125.5 2.3 constant_dynamic-update-slice_fusion.5
  127.7 3.0 collective-permute-start.5
  130.8 1.1 constant_dynamic-update-slice_fusion.4
  131.8 43.3 %collective-permute-done.4 = bf16[512,1024]{1,0:T(8,128)(2,1)} collective-permute-done((bf16[512,1024]{1,0:T(8,128)(2,1)S(1)}, bf16[512,1024]{1,0:T(8,128)(2,1)}, u32[]{:S(2)}, u32[]{:S(2)}) %collective-permute-start.4) | collective-permute-done | bytes 1048608 | tf_op jit(solution)/shard_map/ppermute | solution.py:22
  175.1 3.4 collective-permute-start.6
  178.5 84.1 %all-gather.9.cloned.1.call-done = bf16[4096,1024]{1,0:T(8,128)(2,1)} async-done(((bf16[512,1024]{1,0:T(8,128)(2,1)}), bf16[4096,1024]{1,0:T(8,128)(2,1)}) %all-gather.9.cloned.1.call-update) | async-done | bytes 8388624 | tf_op jit(solution)/shard_map/all_gather | solution.py:61
  262.6 13.8 %convolution_convert_fusion = bf16[1024,1024]{0,1:T(8,128)(2,1)S(1)} fusion(bf16[1024,4096]{1,0:T(8,128)(2,1)} %all-gather.5.cloned.1.call-done, bf16[4096,1024]{1,0:T(8,128)(2,1)} %all-gather.9.cloned.1.call-done), kind=kOutput, calls=%fused_computation.7 | convolution fusion | flops 8590983168 | bytes 18874368 | tf_op jit(solution)/shard_map/dot_general | solution.py:35
  276.3 111.7 %all-gather.7.cloned.1.call-done = bf16[4096,1024]{1,0:T(8,128)(2,1)} async-done(((bf16[512,1024]{1,0:T(8,128)(2,1)}), bf16[4096,1024]{1,0:T(8,128)(2,1)}) %all-gather.7.cloned.1.call-update) | async-done | bytes 8388624 | tf_op jit(solution)/shard_map/all_gather | solution.py:60
  388.0 13.7 %convolution_convert_fusion.1 = bf16[1024,1024]{0,1:T(8,128)(2,1)S(1)} fusion(bf16[1024,4096]{1,0:T(8,128)(2,1)} %all-gather.5.cloned.1.call-done, bf16[4096,1024]{1,0:T(8,128)(2,1)} %all-gather.7.cloned.1.call-done), kind=kOutput, calls=%fused_computation.8 | convolution fusion | flops 8590983168 | bytes 18874368 | tf_op jit(solution)/shard_map/dot_general | solution.py:35
  401.8 2.5 pad_maximum_fusion
  404.3 6.6 %copy.12 = bf16[1024,2048]{1,0:T(8,128)(2,1)} copy(bf16[1024,2048]{0,1:T(8,128)(2,1)} %pad_maximum_fusion) | data formatting | bytes 8388608 | tf_op jit(solution)/shard_map/concatenate | solution.py:62
  410.9 3.8 gather_fusion
  414.6 3.7 all-to-all-start
  418.4 1.1 constant_dynamic-update-slice_fusion.3
  419.4 2.3 constant_dynamic-update-slice_fusion.2
  421.7 2.3 constant_dynamic-update-slice_fusion.1
  424.0 2.3 constant_dynamic-update-slice_fusion
  426.3 9.1 %fusion.3 = bf16[512,1024]{0,1:T(8,128)(2,1)S(1)} fusion(bf16[4096,1024]{1,0:T(8,128)(2,1)} %constant_dynamic-update-slice_fusion, bf16[512,4096]{1,0:T(8,128)(2,1)} %all-gather.11.cloned.1.call-done), kind=kOutput, calls=%fused_computation.13 | convolution fusion | flops 4295491584 | bytes 13631488 | tf_op jit(solution)/shard_map/dot_general | solution.py:35
  435.4 0.5 copy.16
  436.0 0.3 copy.24
  436.3 7.5 %all-to-all-done = bf16[8,2,16,2048]{3,2,1,0:T(8,128)(2,1)S(1)} async-done(((bf16[8,2,16,2048]{3,2,1,0:T(8,128)(2,1)}), bf16[8,2,16,2048]{3,2,1,0:T(8,128)(2,1)S(1)}, u32[]{:S(2)}, u32[]{:S(2)}) %all-to-all-start) | async-done | bytes 1048608 | tf_op jit(solution)/shard_map/all_to_all | solution.py:67
  443.8 6.2 %gather_fusion.1 = bf16[128,16,2048]{2,1,0:T(8,128)(2,1)} fusion(bf16[16,16,2048]{2,1,0:T(8,128)(2,1)S(1)} %bitcast.30, s32[1024]{0:T(1024)S(1)} %pad_clamp_fusion), kind=kCustom, calls=%fused_computation.1 | custom fusion | bytes 16777728 | tf_op jit(solution)/shard_map/gather | solution.py:69
  450.0 6.0 %fusion.17 = (bf16[16,128,1024]{2,1,0:T(8,128)(2,1)}, bf16[16,128,1024]{2,1,0:T(8,128)(2,1)}) fusion(bf16[16,128,2048]{2,1,0:T(8,128)(2,1)} %bitcast.31), kind=kLoop, calls=%fused_computation.43 | loop fusion | bytes 16777216 | tf_op jit(solution)/shard_map/slice | solution.py:70
  456.0 6.4 %copy.17 = bf16[16,128,1024]{1,2,0:T(8,128)(2,1)} copy(bf16[16,128,1024]{2,1,0:T(8,128)(2,1)} %get-tuple-element.5) | data formatting | bytes 8388608 | tf_op jit(solution)/shard_map/slice | solution.py:70
  462.5 6.4 %copy.15 = bf16[16,128,1024]{1,2,0:T(8,128)(2,1)} copy(bf16[16,128,1024]{2,1,0:T(8,128)(2,1)} %get-tuple-element.6) | data formatting | bytes 8388608 | tf_op jit(solution)/shard_map/slice | solution.py:71
  468.9 3.4 fusion.4
  472.3 1.4 copy-done
  473.6 1.2 fusion.18
  474.8 10.1 %fusion.2 = bf16[16,32,8,128]{3,1,2,0:T(8,128)(2,1)S(1)} fusion(bf16[16,128,8,128]{1,3,2,0:T(8,128)(2,1)} %bitcast.35, f32[16,8,32]{2,1,0:T(8,128)S(1)} %fusion.18, f32[16,8,32,128]{3,2,1,0:T(8,128)} %copy-done, pred[16,128]{1,0:T(8,128)(4,1)S(1)} %broadcast_compare_fusion), kind=kOutput, calls=%fused_computation.12 | convolution fusion | flops 137367680 | bytes 7358464 | tf_op jit(solution)/shard_map/rhgk,rkhe->rghe/dot_general | solution.py:83
  484.9 0.5 copy.21
  485.3 1.2 copy.29
  (26 shorter events, 0.3 us)
Async XLA Ops:
  6.5 2.3 copy-start.1
  6.5 52.8 %copy-start.2 = (s32[16,8]{0,1:T(8,128)S(1)}, s32[16,8]{0,1:T(8,128)}, u32[]{:S(2)}) copy-start(s32[16,8]{0,1:T(8,128)} %param.14) | copy-start | bytes 1540
  6.5 55.9 %copy-start.3 = (s32[1,8,2]{1,2,0:T(2,128)S(1)}, s32[1,8,2]{1,2,0:T(2,128)}, u32[]{:S(2)}) copy-start(s32[1,8,2]{1,2,0:T(2,128)} %param.13) | copy-start | bytes 196
  6.5 172.0 %all-gather.5.cloned.1.call-start = ((), (), s32[]{:S(2)}) async-start(), calls=%async_computation.1 | async-start | bytes 10485760 | tf_op jit(solution)/shard_map/all_gather | solution.py:55
  7.3 255.3 %all-gather.9.cloned.1.call-start = ((), (), s32[]{:S(2)}) async-start(), calls=%async_computation.3 | async-start | bytes 9437184 | tf_op jit(solution)/shard_map/all_gather | solution.py:61
  8.0 380.0 %all-gather.7.cloned.1.call-start = ((), (), s32[]{:S(2)}) async-start(), calls=%async_computation.2 | async-start | bytes 9437184 | tf_op jit(solution)/shard_map/all_gather | solution.py:60
  8.7 417.6 %all-gather.11.cloned.1.call-start = ((), (), s32[]{:S(2)}) async-start(), calls=%async_computation.4 | async-start | bytes 5242880 | tf_op jit(solution)/shard_map/all_gather | solution.py:52
  8.8 47.9 %collective-permute-start = (bf16[512,1024]{1,0:T(8,128)(2,1)S(1)}, bf16[512,1024]{1,0:T(8,128)(2,1)}, u32[]{:S(2)}, u32[]{:S(2)}) collective-permute-start(bf16[512,1024]{1,0:T(8,128)(2,1)S(1)} %copy-done.1), channel_id=1, source_target_pairs={{0,4},{4,8},{8,12},{12,16},{16,20},{20,24},{24,28},{28,0},{1,5},{5... | collective-permute-start | bytes 3145736 | tf_op jit(solution)/shard_map/ppermute | solution.py:22
  11.8 47.5 %collective-permute-start.1 = (bf16[512,1024]{1,0:T(8,128)(2,1)S(1)}, bf16[512,1024]{1,0:T(8,128)(2,1)}, u32[]{:S(2)}, u32[]{:S(2)}) collective-permute-start(bf16[512,1024]{1,0:T(8,128)(2,1)S(1)} %copy-done.1), channel_id=1, source_target_pairs={{0,28},{4,0},{8,4},{12,8},{16,12},{20,16},{24,20},{28,24},{1,29},{... | collective-permute-start | bytes 3145736 | tf_op jit(solution)/shard_map/ppermute | solution.py:27
  56.7 58.2 %collective-permute-start.2 = (bf16[512,1024]{1,0:T(8,128)(2,1)}, bf16[512,1024]{1,0:T(8,128)(2,1)S(1)}, u32[]{:S(2)}, u32[]{:S(2)}) collective-permute-start(bf16[512,1024]{1,0:T(8,128)(2,1)} %collective-permute-done), channel_id=1, source_target_pairs={{0,4},{4,8},{8,12},{12,16},{16,20},{20,24},{24,28},{28,0},{1,5},{5... | collective-permute-start | bytes 3145736 | tf_op jit(solution)/shard_map/ppermute | solution.py:22
  59.4 68.4 %collective-permute-start.3 = (bf16[512,1024]{1,0:T(8,128)(2,1)}, bf16[512,1024]{1,0:T(8,128)(2,1)S(1)}, u32[]{:S(2)}, u32[]{:S(2)}) collective-permute-start(bf16[512,1024]{1,0:T(8,128)(2,1)} %collective-permute-done.1), channel_id=1, source_target_pairs={{0,28},{4,0},{8,4},{12,8},{16,12},{20,16},{24,20},{28,24},{1,29},{... | collective-permute-start | bytes 3145736 | tf_op jit(solution)/shard_map/ppermute | solution.py:27
  114.9 60.2 %collective-permute-start.4 = (bf16[512,1024]{1,0:T(8,128)(2,1)S(1)}, bf16[512,1024]{1,0:T(8,128)(2,1)}, u32[]{:S(2)}, u32[]{:S(2)}) collective-permute-start(bf16[512,1024]{1,0:T(8,128)(2,1)S(1)} %collective-permute-done.2), channel_id=1, source_target_pairs={{0,4},{4,8},{8,12},{12,16},{16,20},{20,24},{24,28},{28,0},{1,5},{5... | collective-permute-start | bytes 3145736 | tf_op jit(solution)/shard_map/ppermute | solution.py:22
  117.6 5.4 %copy-start.4 = (s32[16]{0:T(128)S(1)}, s32[16]{0:T(128)}, u32[]{:S(2)}) copy-start(s32[16]{0:T(128)} %param.15) | copy-start | bytes 196
  127.7 294.0 %collective-permute-start.5 = (bf16[512,1024]{1,0:T(8,128)(2,1)S(1)}, bf16[512,1024]{1,0:T(8,128)(2,1)}, u32[]{:S(2)}, u32[]{:S(2)}) collective-permute-start(bf16[512,1024]{1,0:T(8,128)(2,1)S(1)} %collective-permute-done.3), channel_id=1, source_target_pairs={{0,28},{4,0},{8,4},{12,8},{16,12},{20,16},{24,20},{28,24},{1,29},{... | collective-permute-start | bytes 3145736 | tf_op jit(solution)/shard_map/ppermute | solution.py:27
  175.1 248.9 %collective-permute-start.6 = (bf16[512,1024]{1,0:T(8,128)(2,1)}, bf16[512,1024]{1,0:T(8,128)(2,1)}, u32[]{:S(2)}, u32[]{:S(2)}) collective-permute-start(bf16[512,1024]{1,0:T(8,128)(2,1)} %collective-permute-done.4), channel_id=1, source_target_pairs={{0,4},{4,8},{8,12},{12,16},{16,20},{20,24},{24,28},{28,0},{1,5},{5... | collective-permute-start | bytes 3145736 | tf_op jit(solution)/shard_map/ppermute | solution.py:22
  414.6 29.1 %all-to-all-start = ((bf16[8,2,16,2048]{3,2,1,0:T(8,128)(2,1)}), bf16[8,2,16,2048]{3,2,1,0:T(8,128)(2,1)S(1)}, u32[]{:S(2)}, u32[]{:S(2)}) async-start(bf16[8,2,16,2048]{3,2,1,0:T(8,128)(2,1)} %bitcast.2), calls=%async_computation | async-start | bytes 2097152 | tf_op jit(solution)/shard_map/all_to_all | solution.py:67
  472.3 1.4 copy-start
Sparse Core Ops, SparseCore 0:
  8.9 60.9 all-gather.4
  72.1 190.4 all-gather.8
  264.7 123.2 all-gather.6
  389.4 32.6 all-gather.10
